TPU v7x, 256 devices: a whole 4x4x8 slice. The times are simulated.
256 devices in a mesh: kv: 8 (over x, core), seq: 32 (over z, y).
Axes of the slice: x: 4, y: 4, z: 8, core: 2. Of those that a mesh axis runs over, the one named last changes fastest.
Arguments:
- hidden_states: bfloat16 [6144, 2048], P('seq')
- attn_gain: float32 [2048], replicated, may hold values from 0.5 to 1.5
- w_q: bfloat16 [2048, 2048], P(None, 'kv')
- w_k: bfloat16 [2048, 512], P(None, 'kv')
- w_v: bfloat16 [2048, 512], P(None, 'kv'), may hold values from -0.125 to 0.125
- w_o: bfloat16 [2048, 2048], P('kv'), may hold values from -0.125 to 0.125
- final_gain: float32 [2048], replicated, may hold values from 0.5 to 1.5
- w_head: bfloat16 [2048, 49408], P(None, ('kv', 'seq'))
- doc_lengths: int32 [26], replicated, may hold values from 1 to 3072, as said below
- target_ids: int32 [6144], replicated, may hold values from 0 to 49154, as said below
- vocab_mask: int32 [49408], P(('kv', 'seq')), may hold values from 0 to 1, as said below
Outputs:
- log_probs: float32 [6144], P('seq')
- entropies: float32 [6144], P('seq')
Inputs may be any that keep to these rules, and one draw needn't show every extreme that they name: `doc_lengths`: they sum to 6144; one is 3072, one more is over 1536, every other is under 64. `target_ids`: each names an entry whose vocab_mask is 1. `vocab_mask`: entries from 49155 on are 0.
All inputs are finite; a program needn't handle non-finite values.
Results may differ from a plain program's by a relative error of at most 0.0045.
Values may be sent and summed in bfloat16 or wider, within the bound.
No kernel may reach another device: no remote copies, remote signals or barrier semaphores. Data moves between devices by JAX's collectives and lax.ppermute only.
A program may use at most 128 MiB of HBM per device.

v0:
```python
import math
import jax
import jax.numpy as jnp
from jax import lax
from jax.sharding import Mesh, PartitionSpec as P

HEAD_DIM = 64
ROPE_THETA = 10000000.0
NORM_EPS = 1e-05
NEG_FILL = -1e30
ATTN_SCALE = 0.015625
RESID_SCALE = 5.0
LOGIT_SCALE = 0.125


def rms_norm(values, gain_vec):
    return (
        values * lax.rsqrt(jnp.mean(values * values, axis=-1, keepdims=True) + NORM_EPS) * gain_vec
    )


def rotate(values, positions):
    half_dim = values.shape[-1] // 2
    inverse = jnp.exp(
        jnp.arange(half_dim, dtype=jnp.float32) * (-2.0 * math.log(ROPE_THETA) / values.shape[-1])
    )
    angles = positions.astype(jnp.float32)[:, None] * inverse[None, :]
    cos_val = jnp.cos(angles)[:, None, :]
    sine_val = jnp.sin(angles)[:, None, :]
    lower_half = values[..., :half_dim]
    upper_half = values[..., half_dim:]
    return jnp.concatenate(
        [
            lower_half * cos_val - upper_half * sine_val,
            upper_half * cos_val + lower_half * sine_val,
        ],
        axis=-1,
    )


def local(
    hidden_states,
    attn_gain,
    w_q,
    w_k,
    w_v,
    w_o,
    final_gain,
    w_head,
    doc_lengths,
    target_ids,
    vocab_mask,
):
    tok_rows = hidden_states.shape[0]
    seq_index = lax.axis_index(("z", "y"))
    kv_local = w_k.shape[1] // HEAD_DIM
    q_local = w_q.shape[1] // HEAD_DIM
    group_size = q_local // kv_local
    key_width = kv_local * HEAD_DIM
    stream = hidden_states.astype(jnp.float32)
    normed_in = rms_norm(stream, attn_gain).astype(jnp.bfloat16)
    queries = jnp.dot(normed_in, w_q, preferred_element_type=jnp.float32)
    key_proj = jnp.dot(normed_in, w_k, preferred_element_type=jnp.float32)
    value_proj = jnp.dot(normed_in, w_v, preferred_element_type=jnp.float32)
    token_pos = seq_index * tok_rows + jnp.arange(tok_rows, dtype=jnp.int32)
    doc_ends = jnp.cumsum(doc_lengths)
    doc_starts = doc_ends - doc_lengths
    doc_start = jnp.max(
        jnp.where(doc_starts[None, :] <= token_pos[:, None], doc_starts[None, :], 0), axis=1
    )
    positions = token_pos - doc_start
    rotated_q = rotate(queries.reshape(tok_rows, q_local, HEAD_DIM), positions).astype(jnp.bfloat16)
    rotated_q = rotated_q.reshape(tok_rows, kv_local, group_size, HEAD_DIM)
    rotated_k = rotate(key_proj.reshape(tok_rows, kv_local, HEAD_DIM), positions).astype(
        jnp.bfloat16
    )
    packed = jnp.concatenate(
        [rotated_k.reshape(tok_rows, key_width), value_proj.astype(jnp.bfloat16)], axis=1
    )
    earliest = doc_start[0]
    latest = token_pos[tok_rows - 1]
    initial = (
        jnp.full((kv_local, group_size, tok_rows), NEG_FILL, jnp.float32),
        jnp.zeros((kv_local, group_size, tok_rows), jnp.float32),
        jnp.zeros((kv_local, group_size, tok_rows, HEAD_DIM), jnp.float32),
    )
    shard_rows = lax.all_gather(packed, ("z", "y"), axis=0, tiled=True)
    offset = jnp.int32(0)
    row_count = shard_rows.shape[0]
    key_pos = jnp.arange(row_count, dtype=jnp.int32)

    def update(current):
        top_score, totals, context_sum = current
        key_rows = shard_rows[:, :key_width].reshape(row_count, kv_local, HEAD_DIM)
        value_rows = shard_rows[:, key_width:].reshape(row_count, kv_local, HEAD_DIM)
        scores = (
            jnp.einsum("tkgd,skd->kgts", rotated_q, key_rows, preferred_element_type=jnp.float32)
            * ATTN_SCALE
        )
        allowed = (key_pos[None, :] >= doc_start[:, None]) & (
            key_pos[None, :] <= token_pos[:, None]
        )
        scores = jnp.where(allowed, scores, NEG_FILL)
        new_top = jnp.maximum(top_score, jnp.max(scores, axis=-1))
        weights = jnp.where(allowed, jnp.exp(scores - new_top[..., None]), 0.0)
        rescale = jnp.exp(top_score - new_top)
        totals = jnp.sum(weights, axis=-1)
        context_sum = jnp.einsum(
            "kgts,skd->kgtd",
            weights.astype(jnp.bfloat16),
            value_rows,
            preferred_element_type=jnp.float32,
        )
        return (new_top, totals, context_sum)

    skip_piece = (offset + row_count <= earliest) | (offset > latest)
    top_score, totals, context_sum = lax.cond(skip_piece, lambda current: current, update, initial)
    context = (
        (context_sum / totals[..., None])
        .transpose(2, 0, 1, 3)
        .reshape(tok_rows, q_local * HEAD_DIM)
        .astype(jnp.bfloat16)
    )
    vocab_local = w_head.shape[1]
    y_count = lax.psum(1, "y")
    z_count = lax.psum(1, "z")
    z_index = lax.axis_index("z")
    y_index = lax.axis_index("y")
    kv_index = lax.axis_index("kv")
    attn_out = lax.psum(jnp.dot(context, w_o, preferred_element_type=jnp.float32), "kv")
    final_in = rms_norm(stream + RESID_SCALE * attn_out, final_gain).astype(jnp.bfloat16)
    head_rows = lax.all_gather(final_in, "y", axis=0, tiled=True)
    group_rows = head_rows.shape[0]
    head_cols = lax.all_gather(w_head, "z", axis=1, tiled=True)
    mask_cols = lax.all_gather(vocab_mask, "z", axis=0, tiled=True)
    live_mask = mask_cols == 1
    shard_ids = (
        kv_index * (z_count * y_count) + jnp.arange(z_count, dtype=jnp.int32) * y_count + y_index
    )
    columns = (
        shard_ids[:, None] * vocab_local + jnp.arange(vocab_local, dtype=jnp.int32)[None, :]
    ).reshape(-1)
    row_ids = lax.dynamic_slice_in_dim(target_ids, z_index * group_rows, group_rows, 0)
    logits = jnp.dot(head_rows, head_cols, preferred_element_type=jnp.float32) * LOGIT_SCALE
    masked = jnp.where(live_mask[None, :], logits, NEG_FILL)
    top_row = jnp.max(masked, axis=1)
    shifted = jnp.where(live_mask[None, :], masked - top_row[:, None], 0.0)
    expw = jnp.where(live_mask[None, :], jnp.exp(shifted), 0.0)
    target = jnp.sum(jnp.where(row_ids[:, None] == columns[None, :], logits, 0.0), axis=1)
    row_stats = jnp.stack([top_row, jnp.sum(expw, axis=1), jnp.sum(expw * shifted, axis=1), target])
    top_all = lax.pmax(row_stats[0], ("kv", "y"))
    rescale = jnp.exp(row_stats[0] - top_all)
    total_all, spread_all, target_all = lax.psum(
        (
            row_stats[1] * rescale,
            rescale * (row_stats[2] + (row_stats[0] - top_all) * row_stats[1]),
            row_stats[3],
        ),
        ("kv", "y"),
    )
    log_prob = target_all - top_all - jnp.log(total_all)
    entropy = jnp.log(total_all) - spread_all / total_all
    log_probs = lax.dynamic_slice_in_dim(log_prob, y_index * tok_rows, tok_rows, 0)
    entropies = lax.dynamic_slice_in_dim(entropy, y_index * tok_rows, tok_rows, 0)
    return (log_probs, entropies)


def solution(mesh):
    kv_size, seq_size = mesh.devices.shape
    z_size = mesh.shape["seq"] // 4 if mesh.shape["seq"] % 4 == 0 else mesh.shape["seq"]
    y_size = seq_size // z_size
    split_mesh = Mesh(mesh.devices.reshape(kv_size, z_size, y_size), ("kv", "z", "y"))
    seq = ("z", "y")
    in_specs = (
        P(seq, None),
        P(),
        P(None, "kv"),
        P(None, "kv"),
        P(None, "kv"),
        P("kv", None),
        P(),
        P(None, ("kv",) + seq),
        P(),
        P(),
        P(("kv",) + seq),
    )
    out_specs = (P(seq), P(seq))
    return jax.shard_map(
        local, mesh=split_mesh, in_specs=in_specs, out_specs=out_specs, check_vma=False
    )
```

profile of v0, /device:TPU:32, one launch (start us, length us, event | category | flops | bytes accessed | tf_op | source)
XLA Modules:
  0.0 449.0 jit_solution(1061210086343181944)
XLA Ops:
  8.1 0.9 copy.22
  10.0 1.4 fusion.16
  11.3 1.6 convolution_bitcast_fusion
  13.0 1.6 convolution_convert_fusion
  14.9 0.7 copy.23
  19.0 75.5 %all-gather.5.cloned.1.call-done = bf16[6144,128]{1,0:T(8,128)(2,1)} async-done(((bf16[192,128]{1,0:T(8,128)(2,1)}), bf16[6144,128]{1,0:T(8,128)(2,1)}) %all-gather.5.cloned.1.call-update) | async-done | bytes 1572880 | tf_op jit(solution)/shard_map/all_gather | solution.py:87
  94.5 21.4 %conditional.1 = (f32[1,4,192]{2,1,0:T(4,128)S(1)}, f32[1,4,192,64]{2,3,1,0:T(8,128)S(1)}) conditional(s32[]{:T(128)} %bitcast.9, (s32[6144]{0:T(1024)S(1)}, s32[6144]{0:T(1024)S(1)}, s32[192]{0:T(256)S(1)}, s32[192]{0:T(256)S(1)}, bf16[6144,128]{1,0:T(8,128)(2,1)}, /*index=5*/bf16[192,1,4,64]{0,3,2,1:T(8,128)(2,1)S(1)}) %tuple.16, () %tuple.17), branch_computations={%region_3.6_spmd, %region_6.7_spmd} | conditional | flops 1272839424 | bytes 66424336 | solution.py:117
  94.5 1.0 compare_and_fusion
  95.5 2.6 copy.25
  98.1 5.0 %fusion = (f32[4,192]{1,0:T(4,128)S(1)}, f32[6144,192,4]{0,1,2:T(8,128)S(1)}) fusion(pred[192,6144]{1,0:T(8,128)(4,1)S(1)} %compare_and_fusion, bf16[192,1,4,64]{0,3,2,1:T(8,128)(2,1)S(1)} %get-tuple-element.16, bf16[6144,128]{0,1:T(8,128)(2,1)} %copy.25), kind=kOutput, calls=%fused_computation.2 | convolution fusion | flops 618134784 | bytes 20941824 | tf_op jit(solution)/shard_map/cond/branch_0_fun/tkgd,skd->kgts/dot_general | solution.py:97
  103.1 6.3 %fusion.7 = f32[1,4,192,64]{2,3,1,0:T(8,128)S(1)} fusion(f32[6144,192,4]{0,1,2:T(8,128)S(1)} %get-tuple-element.42, f32[4,192]{1,0:T(4,128)S(1)} %broadcast_maximum_fusion, pred[192,6144]{1,0:T(8,128)(4,1)S(1)} %compare_and_fusion, bf16[6144,128]{0,1:T(8,128)(2,1)} %copy.25), kind=kOutput, calls=%fused_computation.9 | convolution fusion | flops 627572736 | bytes 21040128 | tf_op jit(solution)/shard_map/cond/branch_0_fun/kgts,skd->kgtd/dot_general | solution.py:108
  109.4 6.5 %fusion.2 = f32[4,192]{1,0:T(4,128)S(1)} fusion(f32[6144,192,4]{0,1,2:T(8,128)S(1)} %get-tuple-element.42, f32[4,192]{1,0:T(4,128)S(1)} %broadcast_maximum_fusion, pred[192,6144]{1,0:T(8,128)(4,1)S(1)} %compare_and_fusion), kind=kLoop, calls=%fused_computation.4 | loop fusion | flops 23592192 | bytes 20060160 | tf_op jit(solution)/shard_map/cond/branch_0_fun/reduce_sum | solution.py:107
  115.9 1.6 fusion.35
  118.4 67.6 %all-reduce.4.cloned.1.call-done = f32[192,2048]{1,0:T(8,128)} async-done(((f32[192,2048]{1,0:T(8,128)}), f32[192,2048]{1,0:T(8,128)}) %all-reduce.4.cloned.1.call-update) | async-done | bytes 1572880 | tf_op jit(solution)/shard_map/psum | solution.py:130
  186.1 1.7 multiply_reduce_fusion.1
  187.8 2.6 multiply_convert_fusion
  191.9 0.8 dynamic_slice.9
  192.9 14.0 %all-reduce = s32[1544]{0:T(1024)S(1)} all-reduce(s32[1544]{0:T(1024)S(1)} %dynamic-update-slice), channel_id=1, replica_groups=mesh['kv'=8,'z'=8,'y'=4] {'z'}, use_global_device_ids=true, to_apply=%add | all-reduce | flops 1544 | bytes 12352
  207.0 7.8 %reshape.284 = bf16[1544,2048]{1,0:T(8,128)(2,1)} reshape(bf16[8,193,2048]{2,1,0:T(8,128)(2,1)} %all-gather.9.cloned.1.call-done) | data formatting | bytes 12648448
  214.8 22.4 %all-gather.7.cloned.1.call-done = bf16[768,2048]{1,0:T(8,128)(2,1)} async-done(((bf16[192,2048]{1,0:T(8,128)(2,1)}), bf16[768,2048]{1,0:T(8,128)(2,1)}) %all-gather.7.cloned.1.call-update) | async-done | bytes 3145744 | tf_op jit(solution)/shard_map/all_gather | solution.py:132
  237.2 9.8 %select_reduce_fusion.1 = (f32[768]{0:T(1024)S(1)}, f32[768,1544]{0,1:T(8,128)}) fusion(pred[1544]{0:T(1024)(128)(4,1)S(1)} %broadcast_compare_fusion, bf16[768,2048]{1,0:T(8,128)(2,1)} %all-gather.7.cloned.1.call-done, bf16[1544,2048]{1,0:T(8,128)(2,1)} %reshape.284), kind=kOutput, calls=%fused_computation.23 | convolution fusion | flops 4860560384 | bytes 14217736 | tf_op jit(solution)/shard_map/dot_general | solution.py:144
  247.0 64.9 %pmax.7 = f32[768]{0:T(1024)S(1)} all-reduce(f32[768]{0:T(1024)S(1)} %get-tuple-element.53), channel_id=1, replica_groups=mesh['kv'=8,'z'=8,'y'=4] {'kv','y'}, use_global_device_ids=true, to_apply=%region_12.13 | all-reduce | flops 768 | bytes 6144 | tf_op jit(solution)/shard_map/pmax | solution.py:151
  311.9 4.5 %multiply_reduce_fusion = (f32[768]{0:T(1024)S(1)}, f32[768]{0:T(1024)S(1)}, f32[768]{0:T(1024)S(1)}) fusion(f32[768,1544]{0,1:T(8,128)} %get-tuple-element.54, f32[768]{0:T(1024)S(1)} %get-tuple-element.53, pred[1544]{0:T(1024)(128)(4,1)S(1)} %broadcast_compare_fusion, s32[1544]{0:T(1024)S(1)} %add.107, s32[768]{0:T(1024)S(1)} %dynamic_slice.9), kind=kLoop, calls=%fused_computation.18 | loop fusion | flops 13041408 | bytes 4766248 | tf_op jit(solution)/shard_map/reduce_sum | solution.py:150
  316.5 123.8 %all-reduce.1 = (f32[768]{0:T(1024)S(1)}, f32[768]{0:T(1024)S(1)}, f32[768]{0:T(1024)S(1)}) all-reduce(f32[768]{0:T(1024)S(1)} %get-tuple-element.37, f32[768]{0:T(1024)S(1)} %get-tuple-element.48, f32[768]{0:T(1024)S(1)} %get-tuple-element.47), channel_id=1, replica_groups=mesh['kv'=8,'z'=8,'y'=4] {'kv','y'}, use_global_device_ids=true, to_apply=%region_10.11 | all-reduce | flops 2304 | bytes 18432 | tf_op jit(solution)/shard_map/psum | solution.py:153
  (54 shorter events, 6.4 us)
Async XLA Ops:
  8.0 107.9 %copy-start = (bf16[256,2048]{1,0:T(8,128)(2,1)S(1)}, bf16[256,2048]{1,0:T(8,128)(2,1)}, u32[]{:S(2)}) copy-start(bf16[256,2048]{1,0:T(8,128)(2,1)} %param.18) | copy-start | bytes 3145732
  8.0 10.3 %copy-start.1 = (bf16[192,2048]{1,0:T(8,128)(2,1)S(1)}, bf16[192,2048]{1,0:T(8,128)(2,1)}, u32[]{:S(2)}) copy-start(bf16[192,2048]{1,0:T(8,128)(2,1)} %param.13) | copy-start | bytes 2359300
  8.0 10.3 %copy-start.5 = (f32[2048]{0:T(1024)S(1)}, f32[2048]{0:T(1024)}, u32[]{:S(2)}) copy-start(f32[2048]{0:T(1024)} %param.14) | copy-start | bytes 24580
  8.0 10.3 %copy-start.4 = (bf16[2048,256]{1,0:T(8,128)(2,1)S(1)}, bf16[2048,256]{1,0:T(8,128)(2,1)}, u32[]{:S(2)}) copy-start(bf16[2048,256]{1,0:T(8,128)(2,1)} %param.15) | copy-start | bytes 3145732
  8.0 86.5 %all-gather.5.cloned.1.call-start = ((), (), s32[]{:S(2)}) async-start(), calls=%async_computation | async-start | bytes 1622016 | tf_op jit(solution)/shard_map/all_gather | solution.py:87
  15.6 170.5 %all-reduce.4.cloned.1.call-start = ((), (), s32[]{:S(2)}) async-start(), calls=%async_computation.1 | async-start | bytes 3145728 | tf_op jit(solution)/shard_map/psum | solution.py:130
  115.9 72.0 %copy-start.2 = (f32[2048]{0:T(1024)S(1)}, f32[2048]{0:T(1024)}, u32[]{:S(2)}) copy-start(f32[2048]{0:T(1024)} %param.19) | copy-start | bytes 24580
  117.6 73.1 %copy-start.6 = (u32[256]{0:T(256)S(1)}, u32[256]{0:T(256)}, u32[]{:S(2)}) copy-start(u32[256]{0:T(256)} %constant.73) | copy-start | bytes 3076
  117.6 75.1 %copy-start.3 = (s32[193]{0:T(256)S(1)}, s32[193]{0:T(256)}, u32[]{:S(2)}) copy-start(s32[193]{0:T(256)} %param.23) | copy-start | bytes 2320
  117.6 89.4 %all-gather.9.cloned.1.call-start = ((), (), s32[]{:S(2)}) async-start(), calls=%async_computation.3 | async-start | bytes 7372800 | tf_op jit(solution)/shard_map/all_gather | solution.py:134
  118.2 119.0 %all-gather.7.cloned.1.call-start = ((), (), s32[]{:S(2)}) async-start(), calls=%async_computation.2 | async-start | bytes 3932160 | tf_op jit(solution)/shard_map/all_gather | solution.py:132
Sparse Core Ops, SparseCore 0:
  15.7 78.7 all-gather.4
  117.7 68.2 all-reduce.3
Sparse Core Ops, SparseCore 1:
  119.9 73.3 all-gather.8
  194.9 42.3 all-gather.6
where the time goes:
time: 450 us; the launch traced here: 449 us
  blocking collectives  203 us (45%)
  waiting for transfers between devices  166 us (37%)
  matrix products  26.6 us (6%)
  other arithmetic  19.3 us (4%)
  between operations  17.7 us (4%)
  local copies, waits for them, and re-layouts  16.2 us (4%)
    psum x1, blocking collectives, local(): lax.psum((row_stats[1] * rescale, rescale * (row_stats[2] + (row_stats[0]...  124 us
    all_gather x1, waiting for transfers between devices, local(): shard_rows = lax.all_gather(packed, ('z', 'y'), axis=0, tiled=True)  75.5 us
    psum x1, waiting for transfers between devices, local(): lax.psum(jnp.dot(context, w_o, preferred_element_type=jnp.float32), 'kv')  67.6 us
    pmax x1, blocking collectives, local(): top_all = lax.pmax(row_stats[0], ('kv', 'y'))  64.9 us
    all_gather x1, waiting for transfers between devices, local(): head_rows = lax.all_gather(final_in, 'y', axis=0, tiled=True)  22.4 us
    unnamed x1, blocking collectives  14 us
    dot_general x1, matrix products, local(): jnp.dot(head_rows, head_cols, preferred_element_type=jnp.float32)  9.77 us
  transfers between devices with their start and end apart: 4, of which 3 were waited for; matrix products, arithmetic and copies ran while one was open for 4% of the time, Pallas kernels for 0%

commit v1 on v0

--- a/solution.py
+++ b/solution.py
@@ -84,7 +84,9 @@
         jnp.zeros((kv_local, group_size, tok_rows), jnp.float32),
         jnp.zeros((kv_local, group_size, tok_rows, HEAD_DIM), jnp.float32),
     )
-    shard_rows = lax.all_gather(packed, ("z", "y"), axis=0, tiled=True)
+    shard_rows = jnp.concatenate(
+        lax.all_to_all(jnp.stack([packed] * lax.axis_size(("z", "y"))), ("z", "y"), 0, 0), axis=0
+    )
     offset = jnp.int32(0)
     row_count = shard_rows.shape[0]
     key_pos = jnp.arange(row_count, dtype=jnp.int32)

time: 450 us -> 428 us (0.951)
  waiting for transfers between devices: 166 us -> 123 us
  starting transfers between devices: 0.35 us -> 11.5 us
  matrix products: 26.6 us -> 35 us
    all_gather x1 -> x0, waiting for transfers between devices: 75.5 us -> none  [local(): shard_rows = lax.all_gather(packed, ('z', 'y'), axis=0, tiled=True)]
    all_to_all x0 -> x1, waiting for transfers between devices: none -> 33.2 us  [local(): lax.all_to_all(jnp.stack([packed] * lax.axis_size(('z', 'y'))), ('z', 'y'...]
    all_to_all x0 -> x1, starting transfers between devices: none -> 11.4 us  [local(): lax.all_to_all(jnp.stack([packed] * lax.axis_size(('z', 'y'))), ('z', 'y'...]
where the time goes in v1:
time: 428 us
  blocking collectives  203 us (47%)
  waiting for transfers between devices  123 us (29%)
  matrix products  35 us (8%)
  other arithmetic  23 us (5%)
  between operations  17.7 us (4%)
  local copies, waits for them, and re-layouts  14.4 us (3%)
  starting transfers between devices  11.5 us (3%)
    psum x1, blocking collectives, local(): lax.psum((row_stats[1] * rescale, rescale * (row_stats[2] + (row_stats[0]...  124 us
    psum x1, waiting for transfers between devices, local(): lax.psum(jnp.dot(context, w_o, preferred_element_type=jnp.float32), 'kv')  67.3 us
    pmax x1, blocking collectives, local(): top_all = lax.pmax(row_stats[0], ('kv', 'y'))  64.9 us
    all_to_all x1, waiting for transfers between devices, local(): lax.all_to_all(jnp.stack([packed] * lax.axis_size(('z', 'y'))), ('z', 'y'...  33.2 us
    all_gather x1, waiting for transfers between devices, local(): head_rows = lax.all_gather(final_in, 'y', axis=0, tiled=True)  22.2 us
    unnamed x1, blocking collectives  14.2 us
    all_to_all x1, starting transfers between devices, local(): lax.all_to_all(jnp.stack([packed] * lax.axis_size(('z', 'y'))), ('z', 'y'...  11.4 us
    dot_general x1, matrix products, local(): jnp.dot(head_rows, head_cols, preferred_element_type=jnp.float32)  9.79 us
  transfers between devices with their start and end apart: 4, of which 3 were waited for; matrix products, arithmetic and copies ran while one was open for 4% of the time, Pallas kernels for 0%

profile of v1, /device:TPU:32, one launch (start us, length us, event | category | flops | bytes accessed | tf_op | source)
XLA Modules:
  0.0 427.9 jit_solution(12811593413977909261)
XLA Ops:
  8.1 0.9 copy.28
  9.9 1.4 fusion.16
  11.3 1.6 convolution_bitcast_fusion
  12.9 1.6 convolution_convert_fusion
  14.9 1.5 stack.2
  16.4 11.4 %all-to-all-start = ((bf16[32,192,128]{2,1,0:T(8,128)(2,1)}), bf16[32,192,128]{2,1,0:T(8,128)(2,1)S(1)}, u32[]{:S(2)}, u32[]{:S(2)}) async-start(bf16[32,192,128]{2,1,0:T(8,128)(2,1)} %stack.2), calls=%async_computation | async-start | bytes 3145728 | tf_op jit(solution)/shard_map/all_to_all | solution.py:88
  30.4 1.8 fusion.31
  33.0 33.2 %all-to-all-done = bf16[32,192,128]{2,1,0:T(8,128)(2,1)S(1)} async-done(((bf16[32,192,128]{2,1,0:T(8,128)(2,1)}), bf16[32,192,128]{2,1,0:T(8,128)(2,1)S(1)}, u32[]{:S(2)}, u32[]{:S(2)}) %all-to-all-start) | async-done | bytes 1572896 | tf_op jit(solution)/shard_map/all_to_all | solution.py:88
  66.2 29.0 %conditional.1 = (f32[1,4,192]{2,1,0:T(4,128)S(1)}, f32[1,4,192,64]{2,3,1,0:T(8,128)S(1)}) conditional(s32[]{:T(128)} %bitcast.10, (s32[6144]{0:T(1024)S(1)}, s32[6144]{0:T(1024)S(1)}, s32[192]{0:T(256)S(1)}, s32[192]{0:T(256)S(1)}, bf16[32,192,128]{2,1,0:T(8,128)(2,1)S(1)}, /*index=5*/bf16[192,1,4,64]{0,3,2,1:T(8,128)(2,1)}) %tuple.16, () %tuple.17), branch_computations={%region_3.6_spmd, %region_6.7_spmd} | conditional | flops 1272839424 | bytes 64851472 | solution.py:119
  66.2 1.0 compare_and_fusion
  67.2 9.0 %fusion = (f32[4,192]{1,0:T(4,128)S(1)}, f32[6144,192,4]{0,1,2:T(8,128)}) fusion(pred[192,6144]{1,0:T(8,128)(4,1)S(1)} %compare_and_fusion, bf16[192,1,4,64]{0,3,2,1:T(8,128)(2,1)} %get-tuple-element.17, bf16[6144,128]{1,0:T(8,128)(2,1)S(1)} %bitcast.71), kind=kOutput, calls=%fused_computation.2 | convolution fusion | flops 618134784 | bytes 21728256 | tf_op jit(solution)/shard_map/cond/branch_0_fun/tkgd,skd->kgts/dot_general | solution.py:99
  76.2 9.4 %fusion.8 = f32[1,4,192,64]{2,3,1,0:T(8,128)S(1)} fusion(bf16[6144,128]{1,0:T(8,128)(2,1)S(1)} %bitcast.72, f32[6144,192,4]{0,1,2:T(8,128)} %get-tuple-element.31, f32[4,192]{1,0:T(4,128)S(1)} %broadcast_maximum_fusion, pred[192,6144]{1,0:T(8,128)(4,1)S(1)} %compare_and_fusion), kind=kOutput, calls=%fused_computation.12 | convolution fusion | flops 627572736 | bytes 21826560 | tf_op jit(solution)/shard_map/cond/branch_0_fun/kgts,skd->kgtd/dot_general | solution.py:110
  85.6 9.6 %fusion.2 = f32[4,192]{1,0:T(4,128)S(1)} fusion(f32[6144,192,4]{0,1,2:T(8,128)} %get-tuple-element.31, f32[4,192]{1,0:T(4,128)S(1)} %broadcast_maximum_fusion, pred[192,6144]{1,0:T(8,128)(4,1)S(1)} %compare_and_fusion), kind=kLoop, calls=%fused_computation.4 | loop fusion | flops 23592192 | bytes 20060160 | tf_op jit(solution)/shard_map/cond/branch_0_fun/reduce_sum | solution.py:109
  95.3 1.6 fusion.35
  97.6 67.3 %all-reduce.4.cloned.1.call-done = f32[192,2048]{1,0:T(8,128)} async-done(((f32[192,2048]{1,0:T(8,128)}), f32[192,2048]{1,0:T(8,128)}) %all-reduce.4.cloned.1.call-update) | async-done | bytes 1572880 | tf_op jit(solution)/shard_map/psum | solution.py:132
  164.9 1.7 multiply_reduce_fusion.1
  166.7 2.6 multiply_convert_fusion
  171.7 14.2 %all-reduce = s32[1544]{0:T(1024)S(1)} all-reduce(s32[1544]{0:T(1024)S(1)} %dynamic-update-slice), channel_id=1, replica_groups=mesh['kv'=8,'z'=8,'y'=4] {'z'}, use_global_device_ids=true, to_apply=%add | all-reduce | flops 1544 | bytes 12352
  186.0 7.8 %reshape.290 = bf16[1544,2048]{1,0:T(8,128)(2,1)} reshape(bf16[8,193,2048]{2,1,0:T(8,128)(2,1)} %all-gather.6.cloned.1.call-done) | data formatting | bytes 12648448
  193.8 22.2 %all-gather.4.cloned.1.call-done = bf16[768,2048]{1,0:T(8,128)(2,1)} async-done(((bf16[192,2048]{1,0:T(8,128)(2,1)}), bf16[768,2048]{1,0:T(8,128)(2,1)}) %all-gather.4.cloned.1.call-update) | async-done | bytes 3145744 | tf_op jit(solution)/shard_map/all_gather | solution.py:134
  216.1 9.8 %select_reduce_fusion.1 = (f32[768]{0:T(1024)S(1)}, f32[768,1544]{0,1:T(8,128)}) fusion(pred[1544]{0:T(1024)(128)(4,1)S(1)} %broadcast_compare_fusion, bf16[768,2048]{1,0:T(8,128)(2,1)} %all-gather.4.cloned.1.call-done, bf16[1544,2048]{1,0:T(8,128)(2,1)} %reshape.290), kind=kOutput, calls=%fused_computation.23 | convolution fusion | flops 4860560384 | bytes 14217736 | tf_op jit(solution)/shard_map/dot_general | solution.py:146
  225.9 64.9 %pmax.7 = f32[768]{0:T(1024)S(1)} all-reduce(f32[768]{0:T(1024)S(1)} %get-tuple-element.42), channel_id=1, replica_groups=mesh['kv'=8,'z'=8,'y'=4] {'kv','y'}, use_global_device_ids=true, to_apply=%region_12.13 | all-reduce | flops 768 | bytes 6144 | tf_op jit(solution)/shard_map/pmax | solution.py:153
  290.8 4.5 %multiply_reduce_fusion = (f32[768]{0:T(1024)S(1)}, f32[768]{0:T(1024)S(1)}, f32[768]{0:T(1024)S(1)}) fusion(f32[768,1544]{0,1:T(8,128)} %get-tuple-element.43, f32[768]{0:T(1024)S(1)} %get-tuple-element.42, pred[1544]{0:T(1024)(128)(4,1)S(1)} %broadcast_compare_fusion, s32[1544]{0:T(1024)S(1)} %add.107, s32[768]{0:T(1024)S(1)} %dynamic_slice.9), kind=kLoop, calls=%fused_computation.18 | loop fusion | flops 13041408 | bytes 4766248 | tf_op jit(solution)/shard_map/reduce_sum | solution.py:152
  295.3 123.8 %all-reduce.1 = (f32[768]{0:T(1024)S(1)}, f32[768]{0:T(1024)S(1)}, f32[768]{0:T(1024)S(1)}) all-reduce(f32[768]{0:T(1024)S(1)} %get-tuple-element.26, f32[768]{0:T(1024)S(1)} %get-tuple-element.37, f32[768]{0:T(1024)S(1)} %get-tuple-element.36), channel_id=1, replica_groups=mesh['kv'=8,'z'=8,'y'=4] {'kv','y'}, use_global_device_ids=true, to_apply=%region_10.11 | all-reduce | flops 2304 | bytes 18432 | tf_op jit(solution)/shard_map/psum | solution.py:155
  (51 shorter events, 7.1 us)
Async XLA Ops:
  8.0 87.3 %copy-start = (bf16[256,2048]{1,0:T(8,128)(2,1)S(1)}, bf16[256,2048]{1,0:T(8,128)(2,1)}, u32[]{:S(2)}) copy-start(bf16[256,2048]{1,0:T(8,128)(2,1)} %param.18) | copy-start | bytes 3145732
  8.0 22.4 %copy-start.1 = (bf16[192,2048]{1,0:T(8,128)(2,1)S(1)}, bf16[192,2048]{1,0:T(8,128)(2,1)}, u32[]{:S(2)}) copy-start(bf16[192,2048]{1,0:T(8,128)(2,1)} %param.13) | copy-start | bytes 2359300
  8.0 22.4 %copy-start.4 = (f32[2048]{0:T(1024)S(1)}, f32[2048]{0:T(1024)}, u32[]{:S(2)}) copy-start(f32[2048]{0:T(1024)} %param.14) | copy-start | bytes 24580
  16.4 49.8 %all-to-all-start = ((bf16[32,192,128]{2,1,0:T(8,128)(2,1)}), bf16[32,192,128]{2,1,0:T(8,128)(2,1)S(1)}, u32[]{:S(2)}, u32[]{:S(2)}) async-start(bf16[32,192,128]{2,1,0:T(8,128)(2,1)} %stack.2), calls=%async_computation | async-start | bytes 3145728 | tf_op jit(solution)/shard_map/all_to_all | solution.py:88
  27.8 137.1 %all-reduce.4.cloned.1.call-start = ((), (), s32[]{:S(2)}) async-start(), calls=%async_computation.1 | async-start | bytes 3145728 | tf_op jit(solution)/shard_map/psum | solution.py:132
  95.3 71.4 %copy-start.2 = (f32[2048]{0:T(1024)S(1)}, f32[2048]{0:T(1024)}, u32[]{:S(2)}) copy-start(f32[2048]{0:T(1024)} %param.19) | copy-start | bytes 24580
  97.0 72.5 %copy-start.5 = (u32[256]{0:T(256)S(1)}, u32[256]{0:T(256)}, u32[]{:S(2)}) copy-start(u32[256]{0:T(256)} %constant.73) | copy-start | bytes 3076
  97.0 74.5 %copy-start.3 = (s32[193]{0:T(256)S(1)}, s32[193]{0:T(256)}, u32[]{:S(2)}) copy-start(s32[193]{0:T(256)} %param.23) | copy-start | bytes 2320
  97.0 89.0 %all-gather.6.cloned.1.call-start = ((), (), s32[]{:S(2)}) async-start(), calls=%async_computation.3 | async-start | bytes 7372800 | tf_op jit(solution)/shard_map/all_gather | solution.py:136
  97.6 118.5 %all-gather.4.cloned.1.call-start = ((), (), s32[]{:S(2)}) async-start(), calls=%async_computation.2 | async-start | bytes 3932160 | tf_op jit(solution)/shard_map/all_gather | solution.py:134
Sparse Core Ops, SparseCore 0:
  97.1 67.7 all-reduce.3
Sparse Core Ops, SparseCore 1:
  99.3 72.8 all-gather.5
  173.8 42.2 all-gather.3
